TPU v7x, 32 devices: a whole 2x2x4 slice. The times are simulated.
32 devices in a mesh: grp: 4 (over z), exp: 8 (over y, x, core).
Axes of the slice: x: 2, y: 2, z: 4, core: 2. Of those that a mesh axis runs over, the one named last changes fastest.
Arguments:
- cotangent: bfloat16 [4096, 1440], P(('grp', 'exp')), may hold values from -6 to 6
- hidden: bfloat16 [4096, 4, 1440], P(('grp', 'exp')), may hold values from -0.29882812 to 0.29882812
- gates: bfloat16 [4096, 4], P(('grp', 'exp')), may hold values from 0.049804688 to 1
- expert_ids: int32 [4096, 4], P(('grp', 'exp')), may hold values from 0 to 15, all different within a row; in each aligned block of 128 rows (0 to 127, 128 to 255, ...) at most 40 rows name the same one
- group_counts: int32 [4], P('grp'), may hold values from 146 to 1024, as said below
- w_down: bfloat16 [16, 1440, 1440], P('exp', 'grp'), may hold values from -0.15625 to 0.15625
Outputs:
- d_hidden: bfloat16 [4096, 4, 1440], P(('grp', 'exp'))
- d_gate: bfloat16 [4096, 4], P(('grp', 'exp'))
- d_weight: float32 [16, 1440, 1440], P('exp', 'grp')
Inputs may be any that keep to these rules, and one draw needn't show every extreme that they name: `expert_ids`: within the rows of one device no expert is named more than 40 times, and every expert is named somewhere. `group_counts`: some group has all 1024 slots live, and some group only 146.
All inputs are finite; a program needn't handle non-finite values.
Results may differ from a plain program's by a relative error of at most 0.015.
Values may be sent and summed in bfloat16 or wider, within the bound.
No kernel may reach another device: no remote copies, remote signals or barrier semaphores. Data moves between devices by JAX's collectives and lax.ppermute only.
A program may use at most 128 MiB of HBM per device.

v0:
```python
import jax
import jax.numpy as jnp
from jax import lax
from jax.sharding import PartitionSpec as P

LOSS_SCALE = 32768


def body(cotangent, hidden, gates, expert_ids, group_counts, w_down):
    tok = cotangent.shape[0]
    top = expert_ids.shape[1]
    ffw = hidden.shape[2]
    width = cotangent.shape[1]
    n_exp = lax.axis_size("exp")
    exp_dev = w_down.shape[0]
    experts = exp_dev * n_exp
    most = 5 * tok * top // (4 * experts)
    count = group_counts[0]
    first_row = lax.axis_index("exp") * tok
    live = (first_row + jnp.arange(tok, dtype=jnp.int32) < count).astype(jnp.float32)
    total = lax.psum(count.astype(jnp.float32), "grp")
    scale = LOSS_SCALE / total
    weighted = (gates.astype(jnp.float32) * live[:, None]).astype(jnp.bfloat16)
    flat_ids = expert_ids.reshape(-1)
    onehot = (flat_ids[:, None] == jnp.arange(experts, dtype=jnp.int32)[None, :]).astype(jnp.int32)
    rank = jnp.sum((jnp.cumsum(onehot, axis=0) - onehot) * onehot, axis=1)
    target = flat_ids * most + rank
    slot_tok = jnp.arange(tok * top, dtype=jnp.int32) // top
    dy_buf = jnp.zeros((experts * most, width), jnp.bfloat16).at[target].set(cotangent[slot_tok])
    hid_buf = jnp.zeros((experts * most, ffw), jnp.bfloat16).at[target].set(hidden.reshape(-1, ffw))
    gate_buf = jnp.zeros((experts * most,), jnp.bfloat16).at[target].set(weighted.reshape(-1))
    dy_buf = dy_buf.reshape(n_exp, exp_dev * most, width)
    hid_buf = hid_buf.reshape(n_exp, exp_dev * most, ffw)
    gate_buf = gate_buf.reshape(n_exp, exp_dev * most)
    dy_recv, gate_recv = (
        lax.all_to_all(dy_buf, "exp", split_axis=0, concat_axis=0, tiled=True),
        lax.all_to_all(gate_buf, "exp", split_axis=0, concat_axis=0, tiled=True),
    )
    hid_recv = lax.all_to_all(hid_buf, "exp", split_axis=0, concat_axis=0, tiled=True)
    dy_four = dy_recv.reshape(n_exp, exp_dev, most, width)
    hid_four = hid_recv.reshape(n_exp, exp_dev, most, ffw)
    gate_three = gate_recv.reshape(n_exp, exp_dev, most).astype(jnp.float32)
    proj = jnp.einsum(
        "sjmd,jfd->sjmf",
        dy_four,
        lax.all_gather(w_down, "grp", axis=1, tiled=True),
        preferred_element_type=jnp.float32,
    )
    dh_rows = (gate_three[..., None] * proj).astype(jnp.bfloat16)
    inner = jnp.sum(hid_four.astype(jnp.float32) * proj, axis=3).astype(jnp.bfloat16)
    scaled = (gate_three[..., None] * dy_four.astype(jnp.float32)).astype(jnp.bfloat16)
    partial_grad = (
        jnp.einsum("sjmf,sjmd->jfd", hid_four, scaled, preferred_element_type=jnp.float32) * scale
    )
    d_weight = lax.psum_scatter(
        partial_grad.astype(jnp.bfloat16), "grp", scatter_dimension=1, tiled=True
    ).astype(jnp.float32)
    back_dh, back_inner = (
        lax.all_to_all(
            dh_rows.reshape(n_exp, exp_dev * most, ffw),
            "exp",
            split_axis=0,
            concat_axis=0,
            tiled=True,
        ),
        lax.all_to_all(
            inner.reshape(n_exp, exp_dev * most), "exp", split_axis=0, concat_axis=0, tiled=True
        ),
    )
    d_hidden = back_dh.reshape(experts * most, ffw)[target].reshape(tok, top, ffw)
    inner_tok = back_inner.reshape(-1)[target].reshape(tok, top)
    d_gate = (inner_tok.astype(jnp.float32) * live[:, None]).astype(jnp.bfloat16)
    return (d_hidden, d_gate, d_weight)


def solution(mesh):
    in_specs = (
        P(("grp", "exp"), None),
        P(("grp", "exp"), None, None),
        P(("grp", "exp"), None),
        P(("grp", "exp"), None),
        P("grp"),
        P("exp", "grp", None),
    )
    out_specs = (P(("grp", "exp"), None, None), P(("grp", "exp"), None), P("exp", "grp", None))
    return jax.shard_map(body, mesh=mesh, in_specs=in_specs, out_specs=out_specs, check_vma=False)
```

profile of v0, /device:TPU:0, one launch (start us, length us, event | category | flops | bytes accessed | tf_op | source)
XLA Modules:
  0.0 501.5 jit_solution(16202728035999669125)
XLA Ops:
  7.2 0.0 copy-start.3
  7.2 0.0 copy-start.4
  7.2 0.0 copy-start.1
  7.2 0.0 all-gather.2.cloned.1.call-start
  7.2 0.7 all-gather.2.cloned.1.call-update
  7.9 0.0 copy-done.3
  7.9 0.1 copy.45
  8.1 0.1 eq.25
  8.2 0.1 eq.29
  8.3 0.1 copy.44
  8.4 0.1 mul.61
  8.5 1.2 reduce-window.6
  9.7 0.2 slice_reduce_fusion
  10.6 0.0 copy-done.4
  10.6 0.1 copy.49
  10.8 0.1 reshape.204
  10.9 0.1 fusion.14
  11.0 3.8 scatter_custom_fusion
  14.8 0.7 all_to_all.25
  15.5 5.2 %all-to-all-start = ((bf16[8,1,80]{2,1,0:T(2,128)(2,1)}), bf16[8,1,80]{2,1,0:T(2,128)(2,1)S(1)}, u32[]{:S(2)}, u32[]{:S(2)}) async-start(bf16[8,1,80]{2,1,0:T(2,128)(2,1)} %all_to_all.25), calls=%async_computation | async-start | bytes 8192 | tf_op jit(solution)/shard_map/all_to_all | solution.py:37
  20.6 0.0 copy-done.1
  20.6 1.6 copy.55
  22.2 0.8 reshape.220
  23.0 4.5 scatter_custom_fusion.2
  27.5 0.0 all-to-all-done
  27.5 0.0 copy-start.2
  27.5 4.3 all-to-all-start.3
  31.8 0.0 copy-done.2
  31.8 0.2 copy.52
  32.0 9.6 %scatter_custom_fusion.1 = bf16[640,1440]{1,0:T(8,128)(2,1)} fusion(s32[512]{0:T(512)S(1)} %bitcast.59, bf16[128,1440]{1,0:T(8,128)(2,1)S(1)} %copy.52, s32[1024]{0:T(1024)S(1)} %pad_clamp_fusion.1, bf16[]{:T(256)} %constant.15.clone.1), kind=kCustom, calls=%fused_computation.18 | custom fusion | bytes 1843202 | tf_op jit(solution)/shard_map/scatter | solution.py:29
  41.6 15.5 %all-to-all-done.3 = bf16[8,80,1440]{2,1,0:T(8,128)(2,1)S(1)} async-done(((bf16[8,80,1440]{2,1,0:T(8,128)(2,1)}), bf16[8,80,1440]{2,1,0:T(8,128)(2,1)S(1)}, u32[]{:S(2)}, u32[]{:S(2)}) %all-to-all-start.3) | async-done | bytes 1843232 | tf_op jit(solution)/shard_map/all_to_all | solution.py:39
  57.0 4.3 all-to-all-start.1
  61.4 0.0 all-reduce.3.cloned.1.call-start
  61.4 15.4 %psum.7 = f32[]{:T(128)} all-reduce(f32[]{:T(128)S(6)} %convert_element_type.90), channel_id=1, replica_groups=mesh['grp'=4,'exp'=8] {'grp'}, use_global_device_ids=true, to_apply=%region_7.8 | all-reduce | flops 1 | bytes 8 | tf_op jit(solution)/shard_map/psum | solution.py:21
  77.5 0.1 reshape.174
  77.6 9.0 %all-to-all-done.1 = bf16[8,80,1440]{2,1,0:T(8,128)(2,1)} async-done(((bf16[8,80,1440]{2,1,0:T(8,128)(2,1)}), bf16[8,80,1440]{2,1,0:T(8,128)(2,1)}, u32[]{:S(2)}, u32[]{:S(2)}) %all-to-all-start.1) | async-done | bytes 1843232 | tf_op jit(solution)/shard_map/all_to_all | solution.py:36
  86.6 83.1 %all-gather.2.cloned.1.call-done = bf16[2,1440,1440]{2,1,0:T(8,128)(2,1)} async-done(((bf16[2,360,1440]{2,1,0:T(8,128)(2,1)}), bf16[2,1440,1440]{2,1,0:T(8,128)(2,1)}) %all-gather.2.cloned.1.call-update) | async-done | bytes 8294416 | tf_op jit(solution)/shard_map/all_gather | solution.py:46
  169.7 9.6 %fusion.4 = (bf16[8,2,40]{2,0,1:T(8,128)(2,1)S(1)}, bf16[8,2,40,1440]{3,2,0,1:T(8,128)(2,1)}, bf16[8,2,40,1440]{3,2,0,1:T(8,128)(2,1)S(1)}) fusion(bf16[8,2,40,1440]{3,2,1,0:T(8,128)(2,1)S(1)} %bitcast.55, f32[8,2,40]{2,0,1:T(8,128)S(1)} %copy.51, bf16[8,2,40,1440]{3,2,1,0:T(8,128)(2,1)} %bitcast.6, bf16[2,1440,1440]{2,1,0:T(8,128)(2,1)} %all-gather.2.cloned.1.call-done), kind=kOutput, calls=%fused_computation.13 | convolution fusion | flops 2661580288 | bytes 15671040 | tf_op jit(solution)/shard_map/sjmd,jfd->sjmf/dot_general | solution.py:43
  179.3 7.1 %fusion = bf16[2,1440,1440]{2,1,0:T(8,128)(2,1)} fusion(bf16[8,2,40,1440]{3,2,1,0:T(8,128)(2,1)S(1)} %bitcast.56, f32[]{:T(128)S(6)} %div.13, bf16[8,2,40,1440]{3,2,0,1:T(8,128)(2,1)S(1)} %get-tuple-element.17), kind=kOutput, calls=%fused_computation.7 | convolution fusion | flops 2662502400 | bytes 11980804 | tf_op jit(solution)/shard_map/sjmf,sjmd->jfd/dot_general | solution.py:53
  186.3 0.0 copy-start
  186.3 0.0 all-reduce.3.cloned.1.call-update
  186.4 0.7 convert_element_type.95
  187.0 3.7 all-to-all-start.4
  190.7 0.0 copy-done
  190.7 1.5 copy.54
  192.1 3.1 all-to-all-done.4
  195.3 0.0 copy-start.5
  195.3 3.7 all-to-all-start.2
  199.0 0.0 copy-done.5
  199.0 0.6 dynamic-slice
  200.3 0.1 reshape.173
  200.4 3.5 gather_fusion.1
  203.9 0.1 reshape.175
  204.0 0.1 multiply_convert_fusion.1
  204.1 0.7 copy.62
  204.8 19.4 %all-to-all-done.2 = bf16[8,80,1440]{2,1,0:T(8,128)(2,1)S(1)} async-done(((bf16[8,80,1440]{2,1,0:T(8,128)(2,1)}), bf16[8,80,1440]{2,1,0:T(8,128)(2,1)S(1)}, u32[]{:S(2)}, u32[]{:S(2)}) %all-to-all-start.2) | async-done | bytes 1843232 | tf_op jit(solution)/shard_map/all_to_all | solution.py:59
  224.2 2.1 gather_fusion
  226.3 0.4 reshape.169
  226.7 2.4 copy.61
  229.2 261.2 %all-reduce.3.cloned.1.call-done = bf16[2,1440,1440]{2,1,0:T(8,128)(2,1)} async-done(((bf16[2,1440,1440]{2,1,0:T(8,128)(2,1)}), bf16[2,1440,1440]{2,1,0:T(8,128)(2,1)}) %all-reduce.3.cloned.1.call-update) | async-done | bytes 8294416
  490.3 4.3 dynamic-slice_convert_fusion
  (14 shorter events, 0.1 us)
Async XLA Ops:
  7.2 0.8 copy-start.3
  7.2 3.4 copy-start.4
  7.2 13.4 %copy-start.1 = (bf16[128,4,1440]{0,2,1:T(8,128)(2,1)S(1)}, bf16[128,4,1440]{0,2,1:T(8,128)(2,1)}, u32[]{:S(2)}) copy-start(bf16[128,4,1440]{0,2,1:T(8,128)(2,1)} %param.7) | copy-start | bytes 4423684
  7.2 162.5 %all-gather.2.cloned.1.call-start = ((), (), s32[]{:S(2)}) async-start(), calls=%async_computation.5 | async-start | bytes 11059200 | tf_op jit(solution)/shard_map/all_gather | solution.py:46
  15.5 12.0 %all-to-all-start = ((bf16[8,1,80]{2,1,0:T(2,128)(2,1)}), bf16[8,1,80]{2,1,0:T(2,128)(2,1)S(1)}, u32[]{:S(2)}, u32[]{:S(2)}) async-start(bf16[8,1,80]{2,1,0:T(2,128)(2,1)} %all_to_all.25), calls=%async_computation | async-start | bytes 8192 | tf_op jit(solution)/shard_map/all_to_all | solution.py:37
  27.5 4.3 copy-start.2
  27.5 29.6 %all-to-all-start.3 = ((bf16[8,80,1440]{2,1,0:T(8,128)(2,1)}), bf16[8,80,1440]{2,1,0:T(8,128)(2,1)S(1)}, u32[]{:S(2)}, u32[]{:S(2)}) async-start(bf16[8,80,1440]{2,1,0:T(8,128)(2,1)} %bitcast.12), calls=%async_computation.3 | async-start | bytes 3932160 | tf_op jit(solution)/shard_map/all_to_all | solution.py:39
  57.0 29.6 %all-to-all-start.1 = ((bf16[8,80,1440]{2,1,0:T(8,128)(2,1)}), bf16[8,80,1440]{2,1,0:T(8,128)(2,1)}, u32[]{:S(2)}, u32[]{:S(2)}) async-start(bf16[8,80,1440]{2,1,0:T(8,128)(2,1)} %bitcast.5), calls=%async_computation.1 | async-start | bytes 3932160 | tf_op jit(solution)/shard_map/all_to_all | solution.py:36
  61.4 429.0 %all-reduce.3.cloned.1.call-start = ((), (), s32[]{:S(2)}) async-start(), calls=%async_computation.6 | async-start | bytes 17694720
  186.3 4.4 copy-start
  187.0 8.2 %all-to-all-start.4 = ((bf16[8,1,80]{2,1,0:T(2,128)(2,1)}), bf16[8,1,80]{2,1,0:T(2,128)(2,1)S(1)}, u32[]{:S(2)}, u32[]{:S(2)}) async-start(bf16[8,1,80]{2,1,0:T(2,128)(2,1)} %convert_element_type.95), calls=%async_computation.4 | async-start | bytes 8192 | tf_op jit(solution)/shard_map/all_to_all | solution.py:66
  195.3 3.7 copy-start.5
  195.3 28.9 %all-to-all-start.2 = ((bf16[8,80,1440]{2,1,0:T(8,128)(2,1)}), bf16[8,80,1440]{2,1,0:T(8,128)(2,1)S(1)}, u32[]{:S(2)}, u32[]{:S(2)}) async-start(bf16[8,80,1440]{2,1,0:T(8,128)(2,1)} %bitcast.54), calls=%async_computation.2 | async-start | bytes 3932160 | tf_op jit(solution)/shard_map/all_to_all | solution.py:59
Sparse Core Ops, SparseCore 0:
  9.6 160.0 all-gather.1
  186.5 303.8 all-reduce.2
where the time goes:
time: 502 us; the launch traced here: 501 us
  waiting for transfers between devices  392 us (78%)
  local copies, waits for them, and re-layouts  34.2 us (7%)
  starting transfers between devices  21.3 us (4%)
  matrix products  16.6 us (3%)
  between operations  16.3 us (3%)
  blocking collectives  15.4 us (3%)
  other arithmetic  5.77 us (1%)
    unnamed x3, waiting for transfers between devices  262 us
    all_gather x1, waiting for transfers between devices, body(): lax.all_gather(w_down, 'grp', axis=1, tiled=True)  83.1 us
    all_to_all x1, waiting for transfers between devices, body(): lax.all_to_all(dh_rows.reshape(n_exp, exp_dev * most, ffw), 'exp', split_...  19.4 us
    all_to_all x1, waiting for transfers between devices, body(): lax.all_to_all(hid_buf, 'exp', split_axis=0, concat_axis=0, tiled=True)  15.5 us
    psum x1, blocking collectives, body(): total = lax.psum(count.astype(jnp.float32), 'grp')  15.4 us
  transfers between devices with their start and end apart: 7, of which 6 were waited for; matrix products, arithmetic and copies ran while one was open for 7% of the time, Pallas kernels for 0%

commit v1 on v0

--- a/solution.py
+++ b/solution.py
@@ -40,11 +40,36 @@
     dy_four = dy_recv.reshape(n_exp, exp_dev, most, width)
     hid_four = hid_recv.reshape(n_exp, exp_dev, most, ffw)
     gate_three = gate_recv.reshape(n_exp, exp_dev, most).astype(jnp.float32)
+
+    def _answer_scales(row_axis, own_rows):
+        next_value, carry_in, mid_arr = (
+            jax.lax.psum(1, row_axis),
+            jax.lax.axis_index(row_axis),
+            own_rows.shape[1],
+        )
+        taken_in, y = (own_rows, 1)
+        while y < next_value:
+            taken_in = jnp.concatenate(
+                [
+                    taken_in,
+                    jax.lax.ppermute(
+                        taken_in,
+                        axis_name=row_axis,
+                        perm=list(
+                            map(
+                                lambda hop_no: (hop_no, (hop_no - y) % next_value),
+                                range(next_value),
+                            )
+                        ),
+                    ),
+                ],
+                1,
+            )
+            y = 2 * y
+        return jnp.roll(taken_in, carry_in * mid_arr, 1)
+
     proj = jnp.einsum(
-        "sjmd,jfd->sjmf",
-        dy_four,
-        lax.all_gather(w_down, "grp", axis=1, tiled=True),
-        preferred_element_type=jnp.float32,
+        "sjmd,jfd->sjmf", dy_four, _answer_scales("grp", w_down), preferred_element_type=jnp.float32
     )
     dh_rows = (gate_three[..., None] * proj).astype(jnp.bfloat16)
     inner = jnp.sum(hid_four.astype(jnp.float32) * proj, axis=3).astype(jnp.bfloat16)

time: 502 us -> 638 us (1.27)
  blocking collectives: 15.4 us -> 78.1 us
  waiting for transfers between devices: 392 us -> 433 us
  local copies, waits for them, and re-layouts: 34.2 us -> 52.2 us
    ppermute x0 -> x2, waiting for transfers between devices: none -> 118 us  [_answer_scales(): jax.lax.ppermute(taken_in, axis_name=row_axis, perm=list(map(lambda hop_n...]
    all_gather x1 -> x0, waiting for transfers between devices: 83.1 us -> none  [body(): lax.all_gather(w_down, 'grp', axis=1, tiled=True)]
    psum x1, blocking collectives: 15.4 us -> 78.1 us  [body(): total = lax.psum(count.astype(jnp.float32), 'grp')]
    unnamed x3 -> x2, waiting for transfers between devices: 262 us -> 292 us
    all_to_all x1, waiting for transfers between devices: 15.5 us -> 0.01 us  [body(): lax.all_to_all(hid_buf, 'exp', split_axis=0, concat_axis=0, tiled=True)]
    unnamed x18 -> x27, local copies, waits for them, and re-layouts: 5.58 us -> 18.9 us
    all_to_all x1, waiting for transfers between devices: 9.02 us -> 0.01 us  [body(): lax.all_to_all(dy_buf, 'exp', split_axis=0, concat_axis=0, tiled=True)]
    ppermute x0 -> x2, starting transfers between devices: none -> 6.47 us  [_answer_scales(): jax.lax.ppermute(taken_in, axis_name=row_axis, perm=list(map(lambda hop_n...]
  transfers between devices with their start and end apart: 7 -> 8, of which waited for: 6 -> 5; matrix products, arithmetic and copies ran while one was open for 7% -> 8% of each run, Pallas kernels for 0% -> 0%
where the time goes in v1:
time: 638 us; the launch traced here: 637 us
  waiting for transfers between devices  433 us (68%)
  blocking collectives  78.1 us (12%)
  local copies, waits for them, and re-layouts  52.2 us (8%)
  starting transfers between devices  26.8 us (4%)
  matrix products  20.6 us (3%)
  between operations  16.3 us (3%)
  other arithmetic  10.7 us (2%)
    unnamed x2, waiting for transfers between devices  292 us
    ppermute x2, waiting for transfers between devices, _answer_scales(): jax.lax.ppermute(taken_in, axis_name=row_axis, perm=list(map(lambda hop_n...  118 us
    psum x1, blocking collectives, body(): total = lax.psum(count.astype(jnp.float32), 'grp')  78.1 us
    all_to_all x1, waiting for transfers between devices, body(): lax.all_to_all(dh_rows.reshape(n_exp, exp_dev * most, ffw), 'exp', split_...  19.2 us
    unnamed x27, local copies, waits for them, and re-layouts  18.9 us
  transfers between devices with their start and end apart: 8, of which 5 were waited for; matrix products, arithmetic and copies ran while one was open for 8% of the time, Pallas kernels for 0%

profile of v1, /device:TPU:0, one launch (start us, length us, event | category | flops | bytes accessed | tf_op | source)
XLA Modules:
  0.0 637.4 jit_solution(16660515834725999849)
XLA Ops:
  7.2 0.0 copy-start.5
  7.2 0.0 copy-start.6
  7.2 0.0 copy-start.3
  7.2 5.1 collective-permute-start
  12.3 47.7 %collective-permute-done = bf16[2,360,1440]{2,1,0:T(8,128)(2,1)S(1)} collective-permute-done((bf16[2,360,1440]{2,1,0:T(8,128)(2,1)}, bf16[2,360,1440]{2,1,0:T(8,128)(2,1)S(1)}, u32[]{:S(2)}, u32[]{:S(2)}) %collective-permute-start) | collective-permute-done | bytes 2073632 | tf_op jit(solution)/shard_map/ppermute | solution.py:55
  60.0 4.9 pad_maximum_fusion
  64.9 0.0 copy-done.1
  64.9 1.4 collective-permute-start.1
  66.2 0.0 copy-done.5
  66.2 0.1 copy.45
  66.3 0.1 eq.32
  66.4 0.1 eq.28
  66.6 1.2 reduce-window.6
  67.7 0.2 slice_reduce_fusion
  68.0 0.1 copy.44
  68.1 0.1 mul.64
  68.9 0.1 copy.49
  69.0 0.1 reshape.204
  69.2 0.1 fusion.15
  69.3 3.8 scatter_custom_fusion
  73.0 0.7 all_to_all.25
  73.7 3.7 all-to-all-start
  77.5 1.6 copy.55
  79.1 0.8 reshape.220
  79.8 4.5 scatter_custom_fusion.2
  84.4 0.0 all-to-all-done
  84.4 4.5 all-to-all-start.3
  88.9 0.0 copy-start
  88.9 78.1 %psum.7 = f32[]{:T(128)} all-reduce(f32[]{:T(128)S(6)} %convert_element_type.90), channel_id=1, replica_groups=mesh['grp'=4,'exp'=8] {'grp'}, use_global_device_ids=true, to_apply=%region_7.8 | all-reduce | flops 1 | bytes 8 | tf_op jit(solution)/shard_map/psum | solution.py:21
  167.0 0.2 copy.52
  167.2 9.6 %scatter_custom_fusion.1 = bf16[640,1440]{1,0:T(8,128)(2,1)} fusion(s32[512]{0:T(512)S(1)} %bitcast.58, bf16[128,1440]{1,0:T(8,128)(2,1)S(1)} %copy.52, s32[1024]{0:T(1024)S(1)} %pad_clamp_fusion.1, bf16[]{:T(256)} %constant.50.clone.1), kind=kCustom, calls=%fused_computation.20 | custom fusion | bytes 1843202 | tf_op jit(solution)/shard_map/scatter | solution.py:29
  177.5 1.6 constant_dynamic-update-slice_fusion.5
  179.1 0.1 reshape.174
  179.2 0.0 all-to-all-done.3
  179.2 4.3 all-to-all-start.1
  183.5 0.3 all-reduce.3.cloned.1.call-start
  183.8 3.2 constant_dynamic-update-slice_fusion.4
  187.0 70.5 %collective-permute-done.1 = bf16[2,720,1440]{2,1,0:T(8,128)(2,1)} collective-permute-done((bf16[2,720,1440]{2,1,0:T(8,128)(2,1)}, bf16[2,720,1440]{2,1,0:T(8,128)(2,1)}, u32[]{:S(2)}, u32[]{:S(2)}) %collective-permute-start.1) | collective-permute-done | bytes 4147232 | tf_op jit(solution)/shard_map/ppermute | solution.py:55
  257.4 4.6 constant_dynamic-update-slice_fusion.3
  262.1 1.5 constant_dynamic-update-slice_fusion.2
  263.5 0.9 copy-done.2
  264.5 1.5 constant_dynamic-update-slice_fusion.1
  266.0 4.6 constant_dynamic-update-slice_fusion
  270.6 0.0 all-to-all-done.1
  270.6 10.3 %fusion.5 = (bf16[8,2,40]{2,0,1:T(8,128)(2,1)S(1)}, bf16[8,2,40,1440]{3,2,0,1:T(8,128)(2,1)S(1)}, bf16[8,2,40,1440]{3,2,0,1:T(8,128)(2,1)}) fusion(bf16[8,2,40,1440]{3,2,1,0:T(8,128)(2,1)} %bitcast.13, f32[8,2,40]{2,0,1:T(8,128)S(1)} %copy.51, bf16[8,2,40,1440]{3,2,1,0:T(8,128)(2,1)} %bitcast.8, ...), kind=kOutput, calls=%fused_computation.15 | convolution fusion | flops 2661580288 | bytes 18435844 | tf_op jit(solution)/shard_map/sjmd,jfd->sjmf/dot_general | solution.py:71
  280.9 10.3 %fusion = bf16[2,1440,1440]{2,1,0:T(8,128)(2,1)} fusion(bf16[8,2,40,1440]{3,2,1,0:T(8,128)(2,1)} %bitcast.13, f32[]{:T(128)S(6)} %div.13, bf16[8,2,40,1440]{3,2,0,1:T(8,128)(2,1)} %get-tuple-element.17), kind=kOutput, calls=%fused_computation.7 | convolution fusion | flops 2662502400 | bytes 11980804 | tf_op jit(solution)/shard_map/sjmf,sjmd->jfd/dot_general | solution.py:78
  291.2 0.0 all-reduce.3.cloned.1.call-update
  291.2 0.7 convert_element_type.95
  291.9 3.7 all-to-all-start.4
  295.7 1.5 copy.54
  297.1 3.1 all-to-all-done.4
  300.2 3.9 all-to-all-start.2
  304.1 0.6 dynamic-slice
  305.4 0.1 reshape.173
  305.5 3.5 gather_fusion.1
  309.0 0.1 reshape.175
  309.1 0.1 multiply_convert_fusion.1
  309.2 0.7 copy.62
  309.9 19.2 %all-to-all-done.2 = bf16[8,80,1440]{2,1,0:T(8,128)(2,1)S(1)} async-done(((bf16[8,80,1440]{2,1,0:T(8,128)(2,1)}), bf16[8,80,1440]{2,1,0:T(8,128)(2,1)S(1)}, u32[]{:S(2)}, u32[]{:S(2)}) %all-to-all-start.2) | async-done | bytes 1843232 | tf_op jit(solution)/shard_map/all_to_all | solution.py:84
  329.0 2.1 gather_fusion
  331.2 0.4 reshape.169
  331.6 2.4 copy.61
  334.0 292.2 %all-reduce.3.cloned.1.call-done = bf16[2,1440,1440]{2,1,0:T(8,128)(2,1)} async-done(((bf16[2,1440,1440]{2,1,0:T(8,128)(2,1)}), bf16[2,1440,1440]{2,1,0:T(8,128)(2,1)}) %all-reduce.3.cloned.1.call-update) | async-done | bytes 8294416
  626.3 4.3 dynamic-slice_convert_fusion
  (23 shorter events, 0.2 us)
Async XLA Ops:
  7.2 59.1 %copy-start.5 = (s32[128,4]{0,1:T(4,128)S(1)}, s32[128,4]{0,1:T(4,128)}, u32[]{:S(2)}) copy-start(s32[128,4]{0,1:T(4,128)} %param.9) | copy-start | bytes 6148
  7.2 61.7 %copy-start.6 = (bf16[128,4]{0,1:T(4,128)(2,1)S(1)}, bf16[128,4]{0,1:T(4,128)(2,1)}, u32[]{:S(2)}) copy-start(bf16[128,4]{0,1:T(4,128)(2,1)} %param.8) | copy-start | bytes 3076
  7.2 70.3 %copy-start.3 = (bf16[128,4,1440]{0,2,1:T(8,128)(2,1)S(1)}, bf16[128,4,1440]{0,2,1:T(8,128)(2,1)}, u32[]{:S(2)}) copy-start(bf16[128,4,1440]{0,2,1:T(8,128)(2,1)} %param.7) | copy-start | bytes 4423684
  7.2 52.8 %collective-permute-start = (bf16[2,360,1440]{2,1,0:T(8,128)(2,1)}, bf16[2,360,1440]{2,1,0:T(8,128)(2,1)S(1)}, u32[]{:S(2)}, u32[]{:S(2)}) collective-permute-start(bf16[2,360,1440]{2,1,0:T(8,128)(2,1)} %param.11), channel_id=1, source_target_pairs={{0,24},{8,0},{16,8},{24,16},{1,25},{9,1},{17,9},{25,17},{2,26},{10... | collective-permute-start | bytes 6220808 | tf_op jit(solution)/shard_map/ppermute | solution.py:55
  60.0 4.9 copy-start.1
  64.9 192.6 %collective-permute-start.1 = (bf16[2,720,1440]{2,1,0:T(8,128)(2,1)}, bf16[2,720,1440]{2,1,0:T(8,128)(2,1)}, u32[]{:S(2)}, u32[]{:S(2)}) collective-permute-start(bf16[2,720,1440]{2,1,0:T(8,128)(2,1)} %pad_maximum_fusion), channel_id=1, source_target_pairs={{0,16},{8,24},{16,0},{24,8},{1,17},{9,25},{17,1},{25,9},{2,18},{10... | collective-permute-start | bytes 12441608 | tf_op jit(solution)/shard_map/ppermute | solution.py:55
  73.7 10.7 %all-to-all-start = ((bf16[8,1,80]{2,1,0:T(2,128)(2,1)}), bf16[8,1,80]{2,1,0:T(2,128)(2,1)S(1)}, u32[]{:S(2)}, u32[]{:S(2)}) async-start(bf16[8,1,80]{2,1,0:T(2,128)(2,1)} %all_to_all.25), calls=%async_computation | async-start | bytes 8192 | tf_op jit(solution)/shard_map/all_to_all | solution.py:37
  84.4 82.6 %copy-start.4 = (bf16[128,1440]{0,1:T(8,128)(2,1)S(1)}, bf16[128,1440]{0,1:T(8,128)(2,1)}, u32[]{:S(2)}) copy-start(bf16[128,1440]{0,1:T(8,128)(2,1)} %param.6) | copy-start | bytes 1105924
  84.4 94.8 %all-to-all-start.3 = ((bf16[8,80,1440]{2,1,0:T(8,128)(2,1)}), bf16[8,80,1440]{2,1,0:T(8,128)(2,1)}, u32[]{:S(2)}, u32[]{:S(2)}) async-start(bf16[8,80,1440]{2,1,0:T(8,128)(2,1)} %bitcast.12), calls=%async_computation.3 | async-start | bytes 3932160 | tf_op jit(solution)/shard_map/all_to_all | solution.py:39
  88.9 88.6 %copy-start = (bf16[2,360,1440]{2,1,0:T(8,128)(2,1)S(1)}, bf16[2,360,1440]{2,1,0:T(8,128)(2,1)}, u32[]{:S(2)}) copy-start(bf16[2,360,1440]{2,1,0:T(8,128)(2,1)} %param.11) | copy-start | bytes 6220804
  179.2 91.4 %all-to-all-start.1 = ((bf16[8,80,1440]{2,1,0:T(8,128)(2,1)}), bf16[8,80,1440]{2,1,0:T(8,128)(2,1)}, u32[]{:S(2)}, u32[]{:S(2)}) async-start(bf16[8,80,1440]{2,1,0:T(8,128)(2,1)} %bitcast.54), calls=%async_computation.1 | async-start | bytes 3932160 | tf_op jit(solution)/shard_map/all_to_all | solution.py:36
  183.5 442.8 %all-reduce.3.cloned.1.call-start = ((), (), s32[]{:S(2)}) async-start(), calls=%async_computation.5 | async-start | bytes 17694720
  262.1 2.4 copy-start.2
  291.9 8.3 %all-to-all-start.4 = ((bf16[8,1,80]{2,1,0:T(2,128)(2,1)}), bf16[8,1,80]{2,1,0:T(2,128)(2,1)S(1)}, u32[]{:S(2)}, u32[]{:S(2)}) async-start(bf16[8,1,80]{2,1,0:T(2,128)(2,1)} %convert_element_type.95), calls=%async_computation.4 | async-start | bytes 8192 | tf_op jit(solution)/shard_map/all_to_all | solution.py:91
  297.1 7.0 %copy-start.7 = (u32[32]{0:T(128)S(1)}, u32[32]{0:T(128)}, u32[]{:S(2)}) copy-start(u32[32]{0:T(128)} %constant.70) | copy-start | bytes 388
  300.2 28.8 %all-to-all-start.2 = ((bf16[8,80,1440]{2,1,0:T(8,128)(2,1)}), bf16[8,80,1440]{2,1,0:T(8,128)(2,1)S(1)}, u32[]{:S(2)}, u32[]{:S(2)}) async-start(bf16[8,80,1440]{2,1,0:T(8,128)(2,1)} %bitcast.55), calls=%async_computation.2 | async-start | bytes 3932160 | tf_op jit(solution)/shard_map/all_to_all | solution.py:84
Sparse Core Ops, SparseCore 0:
  291.3 334.8 all-reduce.2
